TPU v7x, 512 devices: a whole 4x8x8 slice. The times are simulated.
512 devices in a mesh: dp: 64 (over x, z, y_lo), fsdp: 8 (over y_hi, core).
Axes of the slice: x: 4, y: 8 (y_hi: 4, y_lo: 2; y = y_hi * 2 + y_lo), z: 8, core: 2. Of those that a mesh axis runs over, the one named last changes fastest.
Arguments:
- group_qkv: bfloat16 [64, 1024, 6144], P('dp', 'fsdp'), may hold values from -6 to 6
- cache_pool: bfloat16 [8192, 16, 4096], P('dp', None, 'fsdp'), may hold values from -6 to 6
- page_request: int32 [8192], P('dp'), may hold values from 0 to 64, as said below
- request_host: int32 [64], replicated, may hold values from 0 to 63, each once
- out_weight: bfloat16 [2048, 2048], P(('dp', 'fsdp')), may hold values from -0.5 to 0.5
Outputs:
- projected: bfloat16 [64, 1024, 2048], P('dp', 'fsdp')
Inputs may be any that keep to these rules, and one draw needn't show every extreme that they name: `page_request`: within the slots of one dp index, at most 2 pages belong to one request, and some request has exactly 2 pages in the slots of every dp index. A request holds 1 to 15 pages, or 64 to 128 pages. Some slot is empty.
All inputs are finite; a program needn't handle non-finite values.
Results may differ from a plain program's by a relative error of at most 0.0053.
Values may be sent and summed in bfloat16 or wider, within the bound.
No kernel may reach another device: no remote copies, remote signals or barrier semaphores. Data moves between devices by JAX's collectives and lax.ppermute only.
A program may use at most 64 MiB of HBM per device.

v0:
```python
import math
import jax
import jax.numpy as jnp
from jax import lax
from jax.sharding import PartitionSpec as P

HD = 128
PAGE = 16
MOST = 2


def per_device(group_qkv, cache_pool, page_request, request_host, out_weight):
    fsdp_count = lax.axis_size("fsdp")
    requests = request_host.shape[0]
    slot_count = page_request.shape[0]
    tokens_here = group_qkv.shape[1]
    features = cache_pool.shape[2]
    heads_here = features // (2 * HD)
    score_scale = 1.0 / math.sqrt(HD)
    request_ids = jnp.arange(requests, dtype=jnp.int32)
    member = (page_request[:, None] == request_ids[None, :]).astype(jnp.int32)
    slot_rank = jnp.sum(member * (jnp.cumsum(member, axis=0) - 1), axis=1)
    target_host = jnp.sum(member * request_host[None, :], axis=1)
    is_live = jnp.sum(member, axis=1)
    target_slot = jnp.where(is_live > 0, target_host * MOST + slot_rank, -1)
    chosen = target_slot[:, None] == jnp.arange(requests * MOST, dtype=jnp.int32)[None, :]
    flat_pool = cache_pool.reshape(slot_count, PAGE * features)
    packed = jnp.einsum(
        "sp,sf->pf", chosen.astype(jnp.bfloat16), flat_pool, preferred_element_type=jnp.float32
    )
    packed = packed.astype(jnp.bfloat16).reshape(requests, MOST, PAGE, features)
    occupied = jnp.sum(chosen.astype(jnp.int32), axis=0).reshape(requests, MOST)
    arrived, present = (
        lax.all_to_all(packed, "dp", split_axis=0, concat_axis=0, tiled=True),
        lax.all_to_all(occupied, "dp", split_axis=0, concat_axis=0, tiled=True),
    )
    cached = arrived.reshape(requests * MOST * PAGE, heads_here, 2, HD)
    key_cache = cached[:, :, 0]
    value_cache = cached[:, :, 1]
    live_tokens = jnp.repeat(present.reshape(requests * MOST), PAGE) > 0
    local_qkv = group_qkv.reshape(tokens_here, fsdp_count, heads_here * 3 * HD)
    gathered_qkv = lax.all_to_all(local_qkv, "fsdp", split_axis=1, concat_axis=0, tiled=True)
    group_len = tokens_here * fsdp_count
    gathered_qkv = gathered_qkv.reshape(group_len, heads_here, 3, HD)
    queries = gathered_qkv[:, :, 0]
    new_keys = gathered_qkv[:, :, 1]
    new_values = gathered_qkv[:, :, 2]
    block_rows = min(512, group_len)
    block_count = group_len // block_rows
    query_blocks = queries.reshape(block_count, block_rows, heads_here, HD)

    def attend(inputs):
        query_block, first_row = inputs
        cache_scores = (
            jnp.einsum("qhd,khd->hqk", query_block, key_cache, preferred_element_type=jnp.float32)
            * score_scale
        )
        cache_scores = jnp.where(live_tokens[None, None, :], cache_scores, -jnp.inf)
        group_scores = (
            jnp.einsum("qhd,khd->hqk", query_block, new_keys, preferred_element_type=jnp.float32)
            * score_scale
        )
        causal = jnp.arange(group_len)[None, :] <= first_row + jnp.arange(block_rows)[:, None]
        group_scores = jnp.where(causal[None, :, :], group_scores, -jnp.inf)
        row_max = jnp.maximum(jnp.max(cache_scores, axis=2), jnp.max(group_scores, axis=2))
        cache_expo = jnp.exp(cache_scores - row_max[:, :, None])
        group_expo = jnp.exp(group_scores - row_max[:, :, None])
        row_total = jnp.sum(cache_expo, axis=2) + jnp.sum(group_expo, axis=2)
        mixture = jnp.einsum(
            "hqk,khd->qhd",
            cache_expo.astype(jnp.bfloat16),
            value_cache,
            preferred_element_type=jnp.float32,
        )
        mixture = mixture + jnp.einsum(
            "hqk,khd->qhd",
            group_expo.astype(jnp.bfloat16),
            new_values,
            preferred_element_type=jnp.float32,
        )
        result = mixture / jnp.transpose(row_total)[:, :, None]
        return result.astype(jnp.bfloat16).reshape(block_rows, heads_here * HD)

    starts = jnp.arange(block_count, dtype=jnp.int32) * block_rows
    attn_heads = lax.map(attend, (query_blocks, starts)).reshape(group_len, heads_here * HD)
    tokens_attn = lax.all_to_all(attn_heads, "fsdp", split_axis=0, concat_axis=1, tiled=True)
    summed = jnp.dot(
        tokens_attn,
        lax.all_gather(out_weight, ("dp", "fsdp"), axis=0, tiled=True),
        preferred_element_type=jnp.float32,
    )
    return summed.astype(jnp.bfloat16).reshape(1, tokens_here, out_weight.shape[1])


def solution(mesh):
    return jax.shard_map(
        per_device,
        mesh=mesh,
        in_specs=(
            P("dp", "fsdp", None),
            P("dp", None, "fsdp"),
            P("dp"),
            P(),
            P(("dp", "fsdp"), None),
        ),
        out_specs=P("dp", "fsdp", None),
        check_vma=False,
    )
```

profile of v0, /device:TPU:10, one launch (start us, length us, event | category | flops | bytes accessed | tf_op | source)
XLA Modules:
  0.0 906.4 jit_solution(7879001282318499317)
XLA Ops:
  8.2 0.9 select_reduce_fusion.1
  9.9 14.8 %all-to-all-start = ((s32[64,1,2]{2,1,0:T(1,128)}), s32[64,1,2]{2,1,0:T(1,128)S(1)}, u32[]{:S(2)}, u32[]{:S(2)}) async-start(s32[64,1,2]{2,1,0:T(1,128)} %bitcast.9), calls=%async_computation | async-start | bytes 65536 | tf_op jit(solution)/shard_map/all_to_all | solution.py:35
  24.7 2.6 copy.34
  27.3 6.0 all-to-all-done
  33.3 6.2 all-to-all-start.1
  39.5 3.0 copy.49
  43.3 2.2 copy.50
  45.5 33.0 %all-to-all-done.1 = bf16[128,8,768]{0,2,1:T(8,128)(2,1)S(1)} async-done(((bf16[128,8,768]{0,2,1:T(8,128)(2,1)}), bf16[128,8,768]{0,2,1:T(8,128)(2,1)S(1)}, u32[]{:S(2)}, u32[]{:S(2)}) %all-to-all-start.1) | async-done | bytes 1572896 | tf_op jit(solution)/shard_map/all_to_all | solution.py:42
  78.5 8.3 all-to-all-start.2
  87.1 1.0 copy.35
  88.9 1.0 slice_bitcast_fusion
  90.4 45.0 %all-to-all-done.2 = bf16[64,2,16,512]{3,2,1,0:T(8,128)(2,1)} async-done(((bf16[64,2,16,512]{3,2,1,0:T(8,128)(2,1)}), bf16[64,2,16,512]{3,2,1,0:T(8,128)(2,1)}, u32[]{:S(2)}, u32[]{:S(2)}) %all-to-all-start.2) | async-done | bytes 2097184 | tf_op jit(solution)/shard_map/all_to_all | solution.py:34
  135.3 2.5 reshape.84
  137.9 3.9 fusion.42
  142.0 5.8 copy.45
  147.8 27.3 %while.11 = (s32[]{:T(128)}, bf16[2,512,256]{2,1,0:T(8,128)(2,1)S(1)}, bf16[2,512,2,128]{3,1,0,2:T(8,128)(2,1)S(1)}, bf16[2048,2,128]{2,0,1:T(8,128)(2,1)S(1)}, ...) while((s32[]{:T(128)}, ...), condition=%wide.region_10.11_spmd.clone, body=%wide.region_5.10_spmd.clone.sunk | while | flops 1646131712 | bytes 69022040 | solution.py:85
  149.4 2.9 fusion.68
  152.5 1.4 fusion.69
  154.7 1.2 fusion.72
  155.9 1.9 fusion.71
  157.8 1.3 fusion.70
  159.1 2.2 fusion.73
  163.1 2.9 fusion.68
  166.2 1.4 fusion.69
  168.4 1.2 fusion.72
  169.5 1.9 fusion.71
  171.5 1.3 fusion.70
  172.8 2.2 fusion.73
  175.1 20.5 %all_to_all.48 = bf16[8,128,256]{2,1,0:T(8,128)(2,1)S(1)} all-to-all(bf16[8,128,256]{2,1,0:T(8,128)(2,1)S(1)} %bitcast.90), channel_id=1, replica_groups=mesh['dp'=64,'fsdp'=8] {'fsdp'}, dimensions={0} | all-to-all | bytes 1048576 | tf_op jit(solution)/shard_map/all_to_all | solution.py:86
  195.9 685.7 %all-gather.3.cloned.1.call-done = bf16[512,4,2048]{2,1,0:T(4,128)(2,1)} async-done(((bf16[1,4,2048]{2,1,0:T(4,128)(2,1)}), bf16[512,4,2048]{2,1,0:T(4,128)(2,1)}) %all-gather.3.cloned.1.call-update) | async-done | bytes 8388624 | tf_op jit(solution)/shard_map/all_gather | solution.py:89
  881.6 12.5 %reshape.87 = bf16[2048,2048]{1,0:T(8,128)(2,1)} reshape(bf16[512,4,2048]{2,1,0:T(4,128)(2,1)} %all-gather.3.cloned.1.call-done) | data formatting | bytes 16777216
  894.1 5.5 fusion.38
  (49 shorter events, 10.7 us)
Async XLA Ops:
  6.5 875.0 %all-gather.3.cloned.1.call-start = ((), (), s32[]{:S(2)}) async-start(), calls=%async_computation.4 | async-start | bytes 8404992 | tf_op jit(solution)/shard_map/all_gather | solution.py:89
  9.9 23.4 %all-to-all-start = ((s32[64,1,2]{2,1,0:T(1,128)}), s32[64,1,2]{2,1,0:T(1,128)S(1)}, u32[]{:S(2)}, u32[]{:S(2)}) async-start(s32[64,1,2]{2,1,0:T(1,128)} %bitcast.9), calls=%async_computation | async-start | bytes 65536 | tf_op jit(solution)/shard_map/all_to_all | solution.py:35
  33.3 45.2 %all-to-all-start.1 = ((bf16[128,8,768]{0,2,1:T(8,128)(2,1)}), bf16[128,8,768]{0,2,1:T(8,128)(2,1)S(1)}, u32[]{:S(2)}, u32[]{:S(2)}) async-start(bf16[128,8,768]{0,2,1:T(8,128)(2,1)} %bitcast), calls=%async_computation.1 | async-start | bytes 3145728 | tf_op jit(solution)/shard_map/all_to_all | solution.py:42
  78.5 56.8 %all-to-all-start.2 = ((bf16[64,2,16,512]{3,2,1,0:T(8,128)(2,1)}), bf16[64,2,16,512]{3,2,1,0:T(8,128)(2,1)}, u32[]{:S(2)}, u32[]{:S(2)}) async-start(bf16[64,2,16,512]{3,2,1,0:T(8,128)(2,1)} %bitcast.29), calls=%async_computation.2 | async-start | bytes 4194304 | tf_op jit(solution)/shard_map/all_to_all | solution.py:34
  141.8 6.0 copy-start.2
  152.5 2.2 copy-start
  155.9 1.9 copy-start.3
  157.8 1.4 copy-start.1
  166.2 2.2 copy-start
  169.5 1.9 copy-start.3
  171.4 1.4 copy-start.1
Sparse Core Ops, SparseCore 0:
  9.5 871.9 all-gather.2
where the time goes:
time: 907 us; the launch traced here: 906 us
  waiting for transfers between devices  770 us (85%)
  local copies, waits for them, and re-layouts  40.5 us (4%)
  starting transfers between devices  29.3 us (3%)
  matrix products  21.8 us (2%)
  blocking collectives  20.5 us (2%)
  between operations  13.5 us (1%)
  other arithmetic  10.2 us (1%)
    all_gather x1, waiting for transfers between devices, per_device(): lax.all_gather(out_weight, ('dp', 'fsdp'), axis=0, tiled=True)  686 us
    all_to_all x1, waiting for transfers between devices, per_device(): lax.all_to_all(packed, 'dp', split_axis=0, concat_axis=0, tiled=True)  45 us
    all_to_all x1, waiting for transfers between devices, per_device(): lax.all_to_all(local_qkv, 'fsdp', split_axis=1, concat_axis=0, tiled=True)  33 us
    all_to_all x1, blocking collectives, per_device(): lax.all_to_all(attn_heads, 'fsdp', split_axis=0, concat_axis=1, tiled=True)  20.5 us
    unnamed x6, local copies, waits for them, and re-layouts  20.3 us
  transfers between devices with their start and end apart: 4, of which 4 were waited for; matrix products, arithmetic and copies ran while one was open for 6% of the time, Pallas kernels for 0%

commit v1 on v0

--- a/solution.py
+++ b/solution.py
@@ -86,7 +86,15 @@
     tokens_attn = lax.all_to_all(attn_heads, "fsdp", split_axis=0, concat_axis=1, tiled=True)
     summed = jnp.dot(
         tokens_attn,
-        lax.all_gather(out_weight, ("dp", "fsdp"), axis=0, tiled=True),
+        jnp.concatenate(
+            jax.lax.all_to_all(
+                jnp.stack([out_weight for _ in range(jax.lax.axis_size(("dp", "fsdp")))]),
+                ("dp", "fsdp"),
+                split_axis=0,
+                concat_axis=0,
+            ),
+            axis=0,
+        ),
         preferred_element_type=jnp.float32,
     )
     return summed.astype(jnp.bfloat16).reshape(1, tokens_here, out_weight.shape[1])

time: 907 us -> 420 us (0.46)
  the two profiles are of different devices: /device:TPU:10 before, /device:TPU:16 now
where the time goes in v1:
time: 420 us; the launch traced here: 419 us
  waiting for transfers between devices  271 us (65%)
  local copies, waits for them, and re-layouts  54.7 us (13%)
  starting transfers between devices  41.5 us (10%)
  matrix products  21.7 us (5%)
  blocking collectives  19 us (5%)
  other arithmetic  10.3 us (2%)
    all_to_all x1, waiting for transfers between devices, per_device(): jax.lax.all_to_all(jnp.stack([out_weight for _ in range(jax.lax.axis_size...  187 us
    all_to_all x1, waiting for transfers between devices, per_device(): lax.all_to_all(packed, 'dp', split_axis=0, concat_axis=0, tiled=True)  42.1 us
    all_to_all x1, waiting for transfers between devices, per_device(): lax.all_to_all(local_qkv, 'fsdp', split_axis=1, concat_axis=0, tiled=True)  34.2 us
    all_to_all x1, blocking collectives, per_device(): lax.all_to_all(attn_heads, 'fsdp', split_axis=0, concat_axis=1, tiled=True)  19 us
    all_to_all x1, starting transfers between devices, per_device(): lax.all_to_all(occupied, 'dp', split_axis=0, concat_axis=0, tiled=True)  14.8 us
    all_to_all x1, starting transfers between devices, per_device(): jax.lax.all_to_all(jnp.stack([out_weight for _ in range(jax.lax.axis_size...  14.4 us
    reshape x1, local copies, waits for them, and re-layouts, per_device(): jnp.concatenate(jax.lax.all_to_all(jnp.stack([out_weight for _ in range(j...  12.5 us
  transfers between devices with their start and end apart: 4, of which 4 were waited for; matrix products, arithmetic and copies ran while one was open for 4% of the time, Pallas kernels for 0%

profile of v1, /device:TPU:16, one launch (start us, length us, event | category | flops | bytes accessed | tf_op | source)
XLA Modules:
  0.0 418.6 jit_solution(11955380357489103725)
XLA Ops:
  2.8 14.8 %all-to-all-start = ((s32[64,1,2]{2,1,0:T(1,128)}), s32[64,1,2]{2,1,0:T(1,128)S(1)}, u32[]{:S(2)}, u32[]{:S(2)}) async-start(s32[64,1,2]{2,1,0:T(1,128)} %bitcast.9), calls=%async_computation | async-start | bytes 65536 | tf_op jit(solution)/shard_map/all_to_all | solution.py:35
  17.6 2.6 copy.34
  20.2 7.7 %all-to-all-done = s32[64,1,2]{2,1,0:T(1,128)S(1)} async-done(((s32[64,1,2]{2,1,0:T(1,128)}), s32[64,1,2]{2,1,0:T(1,128)S(1)}, u32[]{:S(2)}, u32[]{:S(2)}) %all-to-all-start) | async-done | bytes 544 | tf_op jit(solution)/shard_map/all_to_all | solution.py:35
  27.9 6.5 %all-to-all-start.1 = ((bf16[128,8,768]{0,2,1:T(8,128)(2,1)}), bf16[128,8,768]{0,2,1:T(8,128)(2,1)}, u32[]{:S(2)}, u32[]{:S(2)}) async-start(bf16[128,8,768]{0,2,1:T(8,128)(2,1)} %bitcast), calls=%async_computation.1 | async-start | bytes 3145728 | tf_op jit(solution)/shard_map/all_to_all | solution.py:42
  34.5 1.4 copy.49
  36.7 2.1 copy.50
  38.8 34.2 %all-to-all-done.1 = bf16[128,8,768]{0,2,1:T(8,128)(2,1)} async-done(((bf16[128,8,768]{0,2,1:T(8,128)(2,1)}), bf16[128,8,768]{0,2,1:T(8,128)(2,1)}, u32[]{:S(2)}, u32[]{:S(2)}) %all-to-all-start.1) | async-done | bytes 1572896 | tf_op jit(solution)/shard_map/all_to_all | solution.py:42
  73.0 5.7 %all-to-all-start.2 = ((bf16[64,2,16,512]{3,2,1,0:T(8,128)(2,1)}), bf16[64,2,16,512]{3,2,1,0:T(8,128)(2,1)}, u32[]{:S(2)}, u32[]{:S(2)}) async-start(bf16[64,2,16,512]{3,2,1,0:T(8,128)(2,1)} %bitcast.28), calls=%async_computation.2 | async-start | bytes 4194304 | tf_op jit(solution)/shard_map/all_to_all | solution.py:34
  79.0 3.6 copy.35
  82.6 2.5 reshape.86
  86.7 42.1 %all-to-all-done.2 = bf16[64,2,16,512]{3,2,1,0:T(8,128)(2,1)} async-done(((bf16[64,2,16,512]{3,2,1,0:T(8,128)(2,1)}), bf16[64,2,16,512]{3,2,1,0:T(8,128)(2,1)}, u32[]{:S(2)}, u32[]{:S(2)}) %all-to-all-start.2) | async-done | bytes 2097184 | tf_op jit(solution)/shard_map/all_to_all | solution.py:34
  128.8 4.0 reshape.89
  132.8 6.3 %fusion.42 = (bf16[2048,2,1,128]{3,2,1,0:T(2,128)(2,1)}, bf16[2048,2,1,128]{3,2,1,0:T(2,128)(2,1)S(1)}) fusion(bf16[2048,2,2,128]{3,2,1,0:T(2,128)(2,1)} %reshape.89), kind=kLoop, calls=%fused_computation.51 | loop fusion | bytes 4194304 | tf_op jit(solution)/shard_map/slice | solution.py:39
  139.3 5.8 %copy.45 = bf16[2048,2,1,128]{0,3,1,2:T(8,128)(2,1)} copy(bf16[2048,2,1,128]{3,2,1,0:T(2,128)(2,1)} %get-tuple-element.135) | data formatting | bytes 2097152 | tf_op jit(solution)/shard_map/squeeze | solution.py:39
  145.2 27.2 %while.11 = (s32[]{:T(128)}, bf16[2,512,256]{2,1,0:T(8,128)(2,1)S(1)}, bf16[2,512,2,128]{3,1,0,2:T(8,128)(2,1)S(1)}, bf16[2048,2,128]{2,0,1:T(8,128)(2,1)S(1)}, ...) while((s32[]{:T(128)}, ...), condition=%wide.region_10.11_spmd.clone, body=%wide.region_5.10_spmd.clone.sunk | while | flops 1646131712 | bytes 69022040 | solution.py:85
  146.8 2.8 fusion.68
  149.8 1.4 fusion.69
  153.2 1.9 fusion.71
  155.1 1.3 fusion.70
  156.4 2.2 fusion.73
  160.4 2.8 fusion.68
  163.4 1.4 fusion.69
  165.6 1.2 fusion.72
  166.8 1.9 fusion.71
  168.7 1.3 fusion.70
  170.1 2.2 fusion.73
  172.4 19.0 %all_to_all.53 = bf16[8,128,256]{2,1,0:T(8,128)(2,1)S(1)} all-to-all(bf16[8,128,256]{2,1,0:T(8,128)(2,1)S(1)} %bitcast.88), channel_id=1, replica_groups=mesh['dp'=64,'fsdp'=8] {'fsdp'}, dimensions={0} | all-to-all | bytes 1048576 | tf_op jit(solution)/shard_map/all_to_all | solution.py:86
  191.4 7.5 %stack.2 = bf16[512,4,2048]{2,1,0:T(4,128)(2,1)} broadcast(bf16[4,2048]{1,0:T(4,128)(2,1)S(1)} %copy-done.4), dimensions={1,2} | broadcast | bytes 8404992 | tf_op jit(solution)/shard_map/stack | solution.py:91
  198.9 14.4 %all-to-all-start.4 = ((bf16[512,4,2048]{2,1,0:T(4,128)(2,1)}), bf16[512,4,2048]{2,1,0:T(4,128)(2,1)}, u32[]{:S(2)}, u32[]{:S(2)}) async-start(bf16[512,4,2048]{2,1,0:T(4,128)(2,1)} %stack.2), calls=%async_computation.4 | async-start | bytes 16777216 | tf_op jit(solution)/shard_map/all_to_all | solution.py:90
  213.6 187.0 %all-to-all-done.4 = bf16[512,4,2048]{2,1,0:T(4,128)(2,1)} async-done(((bf16[512,4,2048]{2,1,0:T(4,128)(2,1)}), bf16[512,4,2048]{2,1,0:T(4,128)(2,1)}, u32[]{:S(2)}, u32[]{:S(2)}) %all-to-all-start.4) | async-done | bytes 8388640 | tf_op jit(solution)/shard_map/all_to_all | solution.py:90
  400.7 12.5 %reshape.90 = bf16[2048,2048]{1,0:T(8,128)(2,1)} reshape(bf16[512,4,2048]{2,1,0:T(4,128)(2,1)} %all-to-all-done.4) | data formatting | bytes 16777216 | tf_op jit(solution)/shard_map/reshape | solution.py:89
  413.2 5.5 %fusion.38 = bf16[1,128,2048]{2,1,0:T(8,128)(2,1)} fusion(bf16[128,2048]{0,1:T(8,128)(2,1)S(1)} %bitcast.84, bf16[2048,2048]{1,0:T(8,128)(2,1)} %reshape.90), kind=kOutput, calls=%fused_computation.37 | convolution fusion | flops 1074003968 | bytes 9437184 | tf_op jit(solution)/shard_map/dot_general | solution.py:87
  (51 shorter events, 12.5 us)
Async XLA Ops:
  0.0 34.5 %copy-start.1 = (bf16[128,16,512]{2,1,0:T(8,128)(2,1)S(1)}, bf16[128,16,512]{2,1,0:T(8,128)(2,1)}, u32[]{:S(2)}) copy-start(bf16[128,16,512]{2,1,0:T(8,128)(2,1)} %param.8) | copy-start | bytes 6291460
  2.8 25.1 %all-to-all-start = ((s32[64,1,2]{2,1,0:T(1,128)}), s32[64,1,2]{2,1,0:T(1,128)S(1)}, u32[]{:S(2)}, u32[]{:S(2)}) async-start(s32[64,1,2]{2,1,0:T(1,128)} %bitcast.9), calls=%async_computation | async-start | bytes 65536 | tf_op jit(solution)/shard_map/all_to_all | solution.py:35
  27.9 45.0 %all-to-all-start.1 = ((bf16[128,8,768]{0,2,1:T(8,128)(2,1)}), bf16[128,8,768]{0,2,1:T(8,128)(2,1)}, u32[]{:S(2)}, u32[]{:S(2)}) async-start(bf16[128,8,768]{0,2,1:T(8,128)(2,1)} %bitcast), calls=%async_computation.1 | async-start | bytes 3145728 | tf_op jit(solution)/shard_map/all_to_all | solution.py:42
  73.0 55.9 %all-to-all-start.2 = ((bf16[64,2,16,512]{3,2,1,0:T(8,128)(2,1)}), bf16[64,2,16,512]{3,2,1,0:T(8,128)(2,1)}, u32[]{:S(2)}, u32[]{:S(2)}) async-start(bf16[64,2,16,512]{3,2,1,0:T(8,128)(2,1)} %bitcast.28), calls=%async_computation.2 | async-start | bytes 4194304 | tf_op jit(solution)/shard_map/all_to_all | solution.py:34
  145.2 46.3 %copy-start.4 = (bf16[4,2048]{1,0:T(4,128)(2,1)S(1)}, bf16[4,2048]{1,0:T(4,128)(2,1)}, u32[]{:S(2)}) copy-start(bf16[4,2048]{1,0:T(4,128)(2,1)} %param.11) | copy-start | bytes 49156
  149.8 2.2 copy-start
  153.2 1.9 copy-start.3
  155.1 1.4 copy-start.2
  163.4 2.2 copy-start
  166.8 1.9 copy-start.3
  168.7 1.4 copy-start.2
  198.9 201.8 %all-to-all-start.4 = ((bf16[512,4,2048]{2,1,0:T(4,128)(2,1)}), bf16[512,4,2048]{2,1,0:T(4,128)(2,1)}, u32[]{:S(2)}, u32[]{:S(2)}) async-start(bf16[512,4,2048]{2,1,0:T(4,128)(2,1)} %stack.2), calls=%async_computation.4 | async-start | bytes 16777216 | tf_op jit(solution)/shard_map/all_to_all | solution.py:90
